TPU v7x, 256 devices: a whole 4x4x8 slice. The times are simulated.
256 devices in a mesh: win: 32 (over x, y, core), exp: 8 (over z).
Axes of the slice: x: 4, y: 4, z: 8, core: 2. Of those that a mesh axis runs over, the one named last changes fastest.
Arguments:
- tokens: bfloat16 [16384, 2048], P('win'), may hold values from -9 to 9
- router: bfloat16 [2048, 32], replicated, may hold values from -0.125 to 0.125
- w_in: bfloat16 [32, 2048, 8192], P('win', None, 'exp'), may hold values from -0.125 to 0.125
- w_out: bfloat16 [32, 8192, 2048], P('win', 'exp'), may hold values from -0.0625 to 0.0625
- expert_ids: int32 [16384, 2], P('win'), may hold values from 0 to 31, all different within a row; in each aligned block of 512 rows (0 to 511, 512 to 1023, ...) at most 48 rows name the same one
- offsets: int32 [32], P('win'), may hold values from 0 to 63
Outputs:
- consensus_state: bfloat16 [16384, 2048], P('win', 'exp')
Inputs may be any that keep to these rules, and one draw needn't show every extreme that they name: `expert_ids`: in each window (an aligned block of 512 rows) no expert is named by more than 48 choices, a bound that some block reaches; a token's two experts differ.
All inputs are finite; a program needn't handle non-finite values.
Results may differ from a plain program's by a relative error of at most 0.015.
Values may be sent and summed in bfloat16 or wider, within the bound.
No kernel may reach another device: no remote copies, remote signals or barrier semaphores. Data moves between devices by JAX's collectives and lax.ppermute only.
A program may use at most 128 MiB of HBM per device.

v0:
```python
import math

import jax
import jax.numpy as jnp
from jax import lax
from jax.sharding import PartitionSpec as P

D = 2048
EXPERTS = 32
OV = 256
CAP = 48


def shifted(shard, axis, by):
    count = lax.axis_size(axis)
    pairs = [(i, i + by) for i in range(count) if 0 <= i + by < count]
    return lax.ppermute(shard, axis, pairs)


def shards(tokens, router, w_in, w_out, expert_ids, offsets):
    tok_count = tokens.shape[0]
    win_size = lax.axis_size("win")
    local_experts = w_in.shape[0]
    col_width = D // lax.axis_size("exp")
    flat_ids = expert_ids.reshape(-1)
    expert_order = jnp.arange(EXPERTS, dtype=jnp.int32)
    hit_table = (flat_ids[:, None] == expert_order[None, :]).astype(jnp.int32)
    rank_table = jnp.cumsum(hit_table, axis=0) - 1
    slot_index = jnp.sum(hit_table * rank_table, axis=1)
    slot_target = flat_ids * CAP + slot_index
    token_index = jnp.repeat(jnp.arange(tok_count, dtype=jnp.int32), 2)
    source_table = jnp.full((EXPERTS * CAP,), tok_count, jnp.int32).at[slot_target].set(token_index)
    padded = jnp.concatenate([tokens, jnp.zeros((1, D), tokens.dtype)], axis=0)
    outgoing = padded[source_table].reshape(win_size, local_experts, CAP, D)
    hidden_rows = jnp.einsum(
        "secd,edf->secf",
        lax.all_to_all(outgoing, "win", split_axis=0, concat_axis=0, tiled=True),
        w_in,
        preferred_element_type=jnp.float32,
    )
    hidden_rows = jax.nn.relu(hidden_rows).astype(jnp.bfloat16)
    results = jnp.einsum("secf,efd->secd", hidden_rows, w_out, preferred_element_type=jnp.float32)
    logits = jnp.dot(tokens, router, preferred_element_type=jnp.float32)
    first_hit = expert_ids[:, 0:1] == expert_order[None, :]
    second_hit = expert_ids[:, 1:2] == expert_order[None, :]
    logit_first = jnp.sum(jnp.where(first_hit, logits, 0.0), axis=1, keepdims=True)
    logit_second = jnp.sum(jnp.where(second_hit, logits, 0.0), axis=1, keepdims=True)
    gate_first = jax.nn.sigmoid(logit_first - logit_second)
    gate_second = jax.nn.sigmoid(logit_second - logit_first)
    returned = lax.all_to_all(results, "win", split_axis=0, concat_axis=0, tiled=True)
    flat_rows = returned.reshape(EXPERTS * CAP, returned.shape[-1])
    picked = flat_rows[slot_target].reshape(tok_count, 2, returned.shape[-1])
    expert_sum = lax.psum_scatter(
        gate_first * picked[:, 0] + gate_second * picked[:, 1],
        "exp",
        scatter_dimension=1,
        tiled=True,
    )
    own_cols = lax.dynamic_slice_in_dim(tokens, lax.axis_index("exp") * col_width, col_width, 1)
    layer_state = (own_cols.astype(jnp.float32) + expert_sum).astype(jnp.bfloat16)
    head_rows = layer_state[:OV]
    tail_rows = layer_state[tok_count - OV :]
    previous = shifted(tail_rows, "win", 1)
    contract = (((1,), (1,)), ((), ()))
    partial_scores = lax.dot_general(
        head_rows, previous, contract, preferred_element_type=jnp.float32
    )
    scores = lax.psum(partial_scores.astype(jnp.bfloat16), "exp").astype(jnp.float32)
    row_pos = jnp.arange(OV, dtype=jnp.int32)[:, None]
    col_pos = jnp.arange(OV, dtype=jnp.int32)[None, :]
    distance = jnp.abs(col_pos - row_pos - offsets[0]).astype(jnp.float32) * (8.0 / OV)
    scores = scores / math.sqrt(D) - distance
    weights = jax.nn.softmax(scores, axis=-1).astype(jnp.bfloat16)
    blended = jnp.dot(weights, previous, preferred_element_type=jnp.float32)
    mixed_rows = (0.5 * (head_rows.astype(jnp.float32) + blended)).astype(jnp.bfloat16)
    mixed_rows = jnp.where(lax.axis_index("win") > 0, mixed_rows, head_rows)
    return jnp.concatenate([mixed_rows, layer_state[OV:]], axis=0)


def solution(mesh):
    return jax.shard_map(
        shards,
        mesh=mesh,
        in_specs=(
            P("win", None),
            P(),
            P("win", None, "exp"),
            P("win", "exp", None),
            P("win", None),
            P("win"),
        ),
        out_specs=P("win", "exp"),
        check_vma=False,
    )
```

profile of v0, /device:TPU:1, one launch (start us, length us, event | category | flops | bytes accessed | tf_op | source)
XLA Modules:
  0.0 515.9 jit_solution(12146455405890550260)
XLA Ops:
  6.5 0.0 copy-start
  6.5 0.9 copy.15
  7.4 0.2 eq.67
  7.6 0.2 eq.63
  7.7 0.7 broadcast_multiply_fusion
  8.4 9.0 %reduce-window.6 = s32[32,8,128]{2,1,0:T(8,128)S(1)} reduce-window(s32[32,8,128]{2,1,0:T(8,128)S(1)} %fusion.20, s32[]{:T(128)} %constant.20.clone.1), window={size=1x1x128 pad=0_0x0_0x127_0}, to_apply=%region_2.3 | reduce-window | flops 4161536 | bytes 262148 | tf_op jit(solution)/shard_map/reduce-window
  17.5 0.1 slice.37
  17.6 0.1 copy.17
  17.7 0.1 copy.18
  17.8 0.1 add_add_fusion
  17.9 0.1 copy.14
  18.1 0.2 mul.54
  18.3 0.2 reshape.133
  18.5 4.3 scatter_custom_fusion
  22.9 1.7 concatenate.6
  24.6 7.1 %gather_fusion = bf16[1536,2048]{1,0:T(8,128)(2,1)} fusion(bf16[513,2048]{1,0:T(8,128)(2,1)S(1)} %concatenate.6, s32[2048]{0:T(1024)S(1)} %pad_clamp_fusion), kind=kCustom, calls=%fused_computation | custom fusion | bytes 12589056 | tf_op jit(solution)/shard_map/gather | solution.py:34
  31.7 0.0 copy-start.3
  31.7 81.9 %all_to_all.10 = bf16[32,1,48,2048]{3,2,1,0:T(8,128)(2,1)S(1)} all-to-all(bf16[32,1,48,2048]{3,2,1,0:T(8,128)(2,1)} %bitcast.61), channel_id=1, replica_groups=mesh['win'=32,'exp'=8] {'win'}, dimensions={0} | all-to-all | bytes 12582912 | tf_op jit(solution)/shard_map/all_to_all | solution.py:37
  113.6 0.0 copy-done.3
  113.6 0.0 copy-start.4
  113.6 6.8 %fusion = bf16[32,48,1024]{2,1,0:T(8,128)(2,1)S(1)} fusion(bf16[32,1,48,2048]{3,2,1,0:T(8,128)(2,1)S(1)} %all_to_all.10, bf16[1,2048,1024]{2,1,0:T(8,128)(2,1)S(1)} %copy-done.3), kind=kOutput, calls=%fused_computation.3 | convolution fusion | flops 6442450944 | bytes 13631488 | tf_op jit(solution)/shard_map/secd,edf->secf/dot_general | solution.py:35
  120.5 0.0 copy-done.4
  120.5 9.1 %convolution_bitcast_fusion = f32[32,1,48,2048]{3,2,1,0:T(8,128)} fusion(bf16[1,1024,2048]{2,1,0:T(8,128)(2,1)S(1)} %copy-done.4, bf16[32,48,1024]{2,1,0:T(8,128)(2,1)S(1)} %fusion), kind=kOutput, calls=%fused_computation.6 | convolution fusion | flops 6447169536 | bytes 19922944 | tf_op jit(solution)/shard_map/secf,efd->secd/dot_general | solution.py:42
  129.6 0.0 copy-start.1
  129.6 5.0 all-to-all-start.1
  134.5 0.2 reduce-scatter.2.cloned.1.call-start
  134.8 0.0 copy-done.2
  134.8 0.0 copy-done
  134.8 0.0 copy-done.1
  134.8 0.8 select_reduce_fusion.1
  135.6 172.2 %all-to-all-done.1 = f32[32,1,48,2048]{3,2,1,0:T(8,128)} async-done(((f32[32,1,48,2048]{3,2,1,0:T(8,128)}), f32[32,1,48,2048]{3,2,1,0:T(8,128)}, u32[]{:S(2)}, u32[]{:S(2)}) %all-to-all-start.1) | async-done | bytes 12582944 | tf_op jit(solution)/shard_map/all_to_all | solution.py:50
  307.8 13.6 %gather_fusion.1 = f32[1024,2048]{1,0:T(8,128)} fusion(f32[1536,2048]{1,0:T(8,128)} %bitcast.17, s32[1024]{0:T(1024)S(1)} %broadcast_clamp_fusion), kind=kCustom, calls=%fused_computation.1 | custom fusion | bytes 16781312 | tf_op jit(solution)/shard_map/gather | solution.py:52
  321.4 10.6 %reshape.112 = f32[512,2,2048]{2,1,0:T(2,128)} reshape(f32[1024,2048]{1,0:T(8,128)} %gather_fusion.1) | data formatting | bytes 16777216 | tf_op jit(solution)/shard_map/reshape | solution.py:52
  331.9 11.0 %fusion.27 = (f32[512,1,2048]{2,1,0:T(1,128)S(1)}, f32[512,1,2048]{2,1,0:T(1,128)S(1)}) fusion(f32[512,2,2048]{2,1,0:T(2,128)} %reshape.112), kind=kLoop, calls=%fused_computation.56 | loop fusion | bytes 16777216 | tf_op jit(solution)/shard_map/slice | solution.py:54
  343.0 6.7 %fusion.3 = f32[512,2048]{1,0:T(8,128)} fusion(f32[512,1,2048]{2,1,0:T(1,128)S(1)} %get-tuple-element.8, f32[512,1,2048]{2,1,0:T(1,128)S(1)} %get-tuple-element.7, f32[512]{0:T(512)S(1)} %get-tuple-element.10, f32[512]{0:T(512)S(1)} %get-tuple-element.9), kind=kLoop, calls=%fused_computation.9 | loop fusion | flops 3145728 | bytes 12587008 | tf_op jit(solution)/shard_map/add | solution.py:54
  349.7 0.0 reduce-scatter.2.cloned.1.call-update
  349.8 0.0 all-reduce.3.cloned.1.call-start
  349.8 80.5 %reduce-scatter.2.cloned.1.call-done = f32[512,256]{1,0:T(8,128)} async-done(((f32[512,2048]{1,0:T(8,128)}), f32[512,256]{1,0:T(8,128)}) %reduce-scatter.2.cloned.1.call-update) | async-done | bytes 524304 | tf_op jit(solution)/shard_map/reduce_scatter | solution.py:53
  430.3 1.1 add_convert_fusion
  431.4 3.7 collective-permute-start
  435.2 1.9 collective-permute-done
  437.1 0.9 convolution_convert_fusion
  438.0 0.0 all-reduce.3.cloned.1.call-update
  438.7 66.3 %all-reduce.3.cloned.1.call-done = bf16[256,256]{1,0:T(8,128)(2,1)} async-done(((bf16[256,256]{1,0:T(8,128)(2,1)}), bf16[256,256]{1,0:T(8,128)(2,1)}) %all-reduce.3.cloned.1.call-update) | async-done | bytes 131088 | tf_op jit(solution)/shard_map/psum | solution.py:68
  505.0 1.1 fusion.11
  506.0 1.1 fusion.12
  507.2 1.2 fusion.10
  508.4 0.7 pad_maximum_fusion
  (13 shorter events, 0.2 us)
Async XLA Ops:
  6.5 128.3 %copy-start = (bf16[2048,32]{0,1:T(8,128)(2,1)S(1)}, bf16[2048,32]{0,1:T(8,128)(2,1)}, u32[]{:S(2)}) copy-start(bf16[2048,32]{0,1:T(8,128)(2,1)} %param.7) | copy-start | bytes 393220
  31.7 81.9 %copy-start.3 = (bf16[1,2048,1024]{2,1,0:T(8,128)(2,1)S(1)}, bf16[1,2048,1024]{2,1,0:T(8,128)(2,1)}, u32[]{:S(2)}) copy-start(bf16[1,2048,1024]{2,1,0:T(8,128)(2,1)} %param.8) | copy-start | bytes 12582916
  113.6 6.8 %copy-start.4 = (bf16[1,1024,2048]{2,1,0:T(8,128)(2,1)S(1)}, bf16[1,1024,2048]{2,1,0:T(8,128)(2,1)}, u32[]{:S(2)}) copy-start(bf16[1,1024,2048]{2,1,0:T(8,128)(2,1)} %param.9) | copy-start | bytes 12582916
  129.6 5.2 %copy-start.2 = (s32[512,2]{0,1:T(2,128)S(1)}, s32[512,2]{0,1:T(2,128)}, u32[]{:S(2)}) copy-start(s32[512,2]{0,1:T(2,128)} %param.10) | copy-start | bytes 12292
  129.6 5.2 %copy-start.1 = (bf16[512,2048]{1,0:T(8,128)(2,1)S(1)}, bf16[512,2048]{1,0:T(8,128)(2,1)}, u32[]{:S(2)}) copy-start(bf16[512,2048]{1,0:T(8,128)(2,1)} %param.6) | copy-start | bytes 6291460
  129.6 178.2 %all-to-all-start.1 = ((f32[32,1,48,2048]{3,2,1,0:T(8,128)}), f32[32,1,48,2048]{3,2,1,0:T(8,128)}, u32[]{:S(2)}, u32[]{:S(2)}) async-start(f32[32,1,48,2048]{3,2,1,0:T(8,128)} %convolution_bitcast_fusion), calls=%async_computation.1 | async-start | bytes 25165824 | tf_op jit(solution)/shard_map/all_to_all | solution.py:50
  134.5 295.8 %reduce-scatter.2.cloned.1.call-start = ((), (), s32[]{:S(2)}) async-start(), calls=%async_computation.3 | async-start | bytes 4718592 | tf_op jit(solution)/shard_map/reduce_scatter | solution.py:53
  349.8 155.2 %all-reduce.3.cloned.1.call-start = ((), (), s32[]{:S(2)}) async-start(), calls=%async_computation.4 | async-start | bytes 262144 | tf_op jit(solution)/shard_map/psum | solution.py:68
  431.4 5.7 %collective-permute-start = (bf16[256,256]{1,0:T(8,128)(2,1)S(1)}, bf16[256,256]{1,0:T(8,128)(2,1)S(1)}, u32[]{:S(2)}, u32[]{:S(2)}) collective-permute-start(bf16[256,256]{1,0:T(8,128)(2,1)S(1)} %slice.42), channel_id=1, source_target_pairs={{0,8},{8,16},{16,24},{24,32},{32,40},{40,48},{48,56},{56,64},{64,7... | collective-permute-start | bytes 393224 | tf_op jit(solution)/shard_map/ppermute | solution.py:17
Sparse Core Ops, SparseCore 0:
  349.9 80.3 reduce-scatter.1
  438.1 66.7 all-reduce.2
where the time goes:
time: 521 us; the launch traced here: 516 us
  waiting for transfers between devices  321 us (62%)
  blocking collectives  81.9 us (16%)
  local copies, waits for them, and re-layouts  50.4 us (10%)
  other arithmetic  20.7 us (4%)
  matrix products  18.7 us (4%)
  between operations  14.3 us (3%)
  starting transfers between devices  8.97 us (2%)
    all_to_all x1, waiting for transfers between devices, shards(): lax.all_to_all(results, 'win', split_axis=0, concat_axis=0, tiled=True)  172 us
    all_to_all x1, blocking collectives, shards(): lax.all_to_all(outgoing, 'win', split_axis=0, concat_axis=0, tiled=True)  81.9 us
    reduce_scatter x1, waiting for transfers between devices, shards(): lax.psum_scatter(gate_first * picked[:, 0] + gate_second * picked[:, 1],...  80.5 us
    psum x1, waiting for transfers between devices, shards(): lax.psum(partial_scores.astype(jnp.bfloat16), 'exp').astype(jnp.float32)  66.3 us
    gather x1, local copies, waits for them, and re-layouts, shards(): picked = flat_rows[slot_target].reshape(tok_count, 2, returned.shape[-1])  13.6 us
    slice x1, local copies, waits for them, and re-layouts, shards(): picked[:, 0]  11 us
    reshape x1, local copies, waits for them, and re-layouts, shards(): picked = flat_rows[slot_target].reshape(tok_count, 2, returned.shape[-1])  10.6 us
  transfers between devices with their start and end apart: 4, of which 4 were waited for; matrix products, arithmetic and copies ran while one was open for 0% of the time, Pallas kernels for 0%

commit v1 on v0

--- a/solution.py
+++ b/solution.py
@@ -17,11 +17,37 @@
     return lax.ppermute(shard, axis, pairs)
 
 
+def ring_reduce(blocks, axis, step):
+    count = blocks.shape[1]
+    me = lax.axis_index(axis)
+    perm = [(i, (i + step) % count) for i in range(count)]
+
+    def take(k):
+        idx = (me - step * k + 2 * count) % count
+        return lax.dynamic_index_in_dim(blocks, idx, axis=1, keepdims=False)
+
+    acc = take(1)
+    for k in range(count - 1):
+        recv = lax.ppermute(acc.astype(jnp.bfloat16), axis, perm)
+        acc = recv.astype(jnp.float32) + take(k + 2)
+    return acc
+
+
+def tree_sum(x, axis):
+    count = lax.axis_size(axis)
+    span = 1
+    while span < count:
+        x = x + lax.ppermute(x, axis, [(i, i ^ span) for i in range(count)])
+        span *= 2
+    return x
+
+
 def shards(tokens, router, w_in, w_out, expert_ids, offsets):
     tok_count = tokens.shape[0]
     win_size = lax.axis_size("win")
+    exp_size = lax.axis_size("exp")
     local_experts = w_in.shape[0]
-    col_width = D // lax.axis_size("exp")
+    col_width = D // exp_size
     flat_ids = expert_ids.reshape(-1)
     expert_order = jnp.arange(EXPERTS, dtype=jnp.int32)
     hit_table = (flat_ids[:, None] == expert_order[None, :]).astype(jnp.int32)
@@ -32,14 +58,19 @@
     source_table = jnp.full((EXPERTS * CAP,), tok_count, jnp.int32).at[slot_target].set(token_index)
     padded = jnp.concatenate([tokens, jnp.zeros((1, D), tokens.dtype)], axis=0)
     outgoing = padded[source_table].reshape(win_size, local_experts, CAP, D)
+    arrived = lax.all_to_all(outgoing, "win", split_axis=0, concat_axis=0, tiled=True)
     hidden_rows = jnp.einsum(
-        "secd,edf->secf",
-        lax.all_to_all(outgoing, "win", split_axis=0, concat_axis=0, tiled=True),
-        w_in,
-        preferred_element_type=jnp.float32,
+        "secd,edf->secf", arrived, w_in, preferred_element_type=jnp.float32
     )
     hidden_rows = jax.nn.relu(hidden_rows).astype(jnp.bfloat16)
     results = jnp.einsum("secf,efd->secd", hidden_rows, w_out, preferred_element_type=jnp.float32)
+    half = col_width // 2
+    blocks = results.reshape(win_size * local_experts * CAP, exp_size, 2, half)
+    reduced = jnp.concatenate(
+        [ring_reduce(blocks[:, :, 0], "exp", 1), ring_reduce(blocks[:, :, 1], "exp", -1)], axis=-1
+    )
+    reduced = reduced.reshape(win_size, local_experts * CAP, col_width)
+    returned = lax.all_to_all(reduced, "win", split_axis=0, concat_axis=0, tiled=True)
     logits = jnp.dot(tokens, router, preferred_element_type=jnp.float32)
     first_hit = expert_ids[:, 0:1] == expert_order[None, :]
     second_hit = expert_ids[:, 1:2] == expert_order[None, :]
@@ -47,15 +78,9 @@
     logit_second = jnp.sum(jnp.where(second_hit, logits, 0.0), axis=1, keepdims=True)
     gate_first = jax.nn.sigmoid(logit_first - logit_second)
     gate_second = jax.nn.sigmoid(logit_second - logit_first)
-    returned = lax.all_to_all(results, "win", split_axis=0, concat_axis=0, tiled=True)
-    flat_rows = returned.reshape(EXPERTS * CAP, returned.shape[-1])
-    picked = flat_rows[slot_target].reshape(tok_count, 2, returned.shape[-1])
-    expert_sum = lax.psum_scatter(
-        gate_first * picked[:, 0] + gate_second * picked[:, 1],
-        "exp",
-        scatter_dimension=1,
-        tiled=True,
-    )
+    flat_rows = returned.reshape(EXPERTS * CAP, col_width)
+    picked = flat_rows[slot_target].reshape(tok_count, 2, col_width)
+    expert_sum = gate_first * picked[:, 0] + gate_second * picked[:, 1]
     own_cols = lax.dynamic_slice_in_dim(tokens, lax.axis_index("exp") * col_width, col_width, 1)
     layer_state = (own_cols.astype(jnp.float32) + expert_sum).astype(jnp.bfloat16)
     head_rows = layer_state[:OV]
@@ -65,7 +90,7 @@
     partial_scores = lax.dot_general(
         head_rows, previous, contract, preferred_element_type=jnp.float32
     )
-    scores = lax.psum(partial_scores.astype(jnp.bfloat16), "exp").astype(jnp.float32)
+    scores = tree_sum(partial_scores, "exp")
     row_pos = jnp.arange(OV, dtype=jnp.int32)[:, None]
     col_pos = jnp.arange(OV, dtype=jnp.int32)[None, :]
     distance = jnp.abs(col_pos - row_pos - offsets[0]).astype(jnp.float32) * (8.0 / OV)

time: 521 us -> 341 us (0.65)
  waiting for transfers between devices: 321 us -> 182 us
  blocking collectives: 81.9 us -> 0 us
  starting transfers between devices: 8.97 us -> 58.5 us
  between operations: 14.3 us -> 1.37 us
  local copies, waits for them, and re-layouts: 50.4 us -> 61.5 us
  other arithmetic: 20.7 us -> 14.5 us
    ppermute x0 -> x17, waiting for transfers between devices: none -> 83.1 us  [the longest x14 49.1 us: ring_reduce(): recv = lax.ppermute(acc.astype(jnp.bfloat16), axis, perm)]
    all_to_all x1 -> x0, blocking collectives: 81.9 us -> none  [shards(): lax.all_to_all(outgoing, 'win', split_axis=0, concat_axis=0, tiled=True)]
    reduce_scatter x1 -> x0, waiting for transfers between devices: 80.5 us -> none  [shards(): lax.psum_scatter(gate_first * picked[:, 0] + gate_second * picked[:, 1],...]
    all_to_all x1 -> x2, waiting for transfers between devices: 172 us -> 97.3 us  [the longest x1 77.1 us: shards(): lax.all_to_all(outgoing, 'win', split_axis=0, concat_axis=0, tiled=True)]
    psum x1 -> x0, waiting for transfers between devices: 66.3 us -> none  [shards(): lax.psum(partial_scores.astype(jnp.bfloat16), 'exp').astype(jnp.float32)]
    ppermute x0 -> x17, starting transfers between devices: none -> 30.5 us  [the longest x14 24 us: ring_reduce(): recv = lax.ppermute(acc.astype(jnp.bfloat16), axis, perm)]
    all_to_all x1 -> x2, starting transfers between devices: 4.97 us -> 26 us  [the longest x1 17.4 us: shards(): lax.all_to_all(reduced, 'win', split_axis=0, concat_axis=0, tiled=True)]
    dynamic_slice x0 -> x1, local copies, waits for them, and re-layouts: none -> 10.8 us  [take(): return lax.dynamic_index_in_dim(blocks, idx, axis=1, keepdims=False)]
  transfers between devices with their start and end apart: 4 -> 20, of which waited for: 4 -> 13; matrix products, arithmetic and copies ran while one was open for 0% -> 1% of each run, Pallas kernels for 0% -> 0%
where the time goes in v1:
time: 341 us; the launch traced here: 340 us
  waiting for transfers between devices  182 us (53%)
  local copies, waits for them, and re-layouts  61.5 us (18%)
  starting transfers between devices  58.5 us (17%)
  matrix products  22 us (6%)
  other arithmetic  14.5 us (4%)
    all_to_all x1, waiting for transfers between devices, shards(): lax.all_to_all(outgoing, 'win', split_axis=0, concat_axis=0, tiled=True)  77.1 us
    ppermute x14, waiting for transfers between devices, ring_reduce(): recv = lax.ppermute(acc.astype(jnp.bfloat16), axis, perm)  49.1 us
    ppermute x3, waiting for transfers between devices, tree_sum(): x = x + lax.ppermute(x, axis, [(i, i ^ span) for i in range(count)])  33.9 us
    ppermute x14, starting transfers between devices, ring_reduce(): recv = lax.ppermute(acc.astype(jnp.bfloat16), axis, perm)  24 us
    all_to_all x1, waiting for transfers between devices, shards(): lax.all_to_all(reduced, 'win', split_axis=0, concat_axis=0, tiled=True)  20.2 us
    all_to_all x1, starting transfers between devices, shards(): lax.all_to_all(reduced, 'win', split_axis=0, concat_axis=0, tiled=True)  17.4 us
    reshape x1, local copies, waits for them, and re-layouts, shards(): blocks = results.reshape(win_size * local_experts * CAP, exp_size, 2, half)  16.9 us
    slice x1, local copies, waits for them, and re-layouts, shards(): blocks[:, :, 0]  13.8 us
  transfers between devices with their start and end apart: 20, of which 13 were waited for; matrix products, arithmetic and copies ran while one was open for 1% of the time, Pallas kernels for 0%

profile of v1, /device:TPU:1, one launch (start us, length us, event | category | flops | bytes accessed | tf_op | source)
XLA Modules:
  0.0 340.2 jit_solution(16704760585121797826)
XLA Ops:
  0.0 0.9 copy.18
  1.2 0.7 broadcast_multiply_fusion
  1.9 9.0 %reduce-window.6 = s32[32,8,128]{2,1,0:T(8,128)S(1)} reduce-window(s32[32,8,128]{2,1,0:T(8,128)S(1)} %fusion.18, s32[]{:T(128)} %constant.202.clone.1), window={size=1x1x128 pad=0_0x0_0x127_0}, to_apply=%region_2.3 | reduce-window | flops 4161536 | bytes 262148 | tf_op jit(solution)/shard_map/reduce-window
  11.5 0.2 mul.54
  12.0 4.3 %scatter_custom_fusion = s32[1536]{0:T(1024)S(1)} fusion(s32[1024]{0:T(1024)S(1)} %bitcast.135, s32[1024]{0:T(1024)S(1)} %reshape.175, s32[]{:T(128)} %constant.209.clone.1), kind=kCustom, calls=%fused_computation.77 | custom fusion | bytes 6148 | tf_op jit(solution)/shard_map/scatter | solution.py:58
  16.3 1.7 concatenate.9
  18.1 7.1 %gather_fusion = bf16[1536,2048]{1,0:T(8,128)(2,1)} fusion(bf16[513,2048]{1,0:T(8,128)(2,1)S(1)} %concatenate.9, s32[2048]{0:T(1024)S(1)} %pad_clamp_fusion), kind=kCustom, calls=%fused_computation | custom fusion | bytes 12589056 | tf_op jit(solution)/shard_map/gather | solution.py:60
  25.2 8.6 %all-to-all-start = ((bf16[32,1,48,2048]{3,2,1,0:T(8,128)(2,1)}), bf16[32,1,48,2048]{3,2,1,0:T(8,128)(2,1)}, u32[]{:S(2)}, u32[]{:S(2)}) async-start(bf16[32,1,48,2048]{3,2,1,0:T(8,128)(2,1)} %bitcast.115), calls=%async_computation | async-start | bytes 12582912 | tf_op jit(solution)/shard_map/all_to_all | solution.py:61
  34.1 77.1 %all-to-all-done = bf16[32,1,48,2048]{3,2,1,0:T(8,128)(2,1)} async-done(((bf16[32,1,48,2048]{3,2,1,0:T(8,128)(2,1)}), bf16[32,1,48,2048]{3,2,1,0:T(8,128)(2,1)}, u32[]{:S(2)}, u32[]{:S(2)}) %all-to-all-start) | async-done | bytes 6291488 | tf_op jit(solution)/shard_map/all_to_all | solution.py:61
  111.1 10.1 %fusion = bf16[32,48,1024]{2,1,0:T(8,128)(2,1)S(1)} fusion(bf16[32,1,48,2048]{3,2,1,0:T(8,128)(2,1)} %all-to-all-done, bf16[1,2048,1024]{2,1,0:T(8,128)(2,1)} %param.8), kind=kOutput, calls=%fused_computation.3 | convolution fusion | flops 6442450944 | bytes 13631488 | tf_op jit(solution)/shard_map/secd,edf->secf/dot_general | solution.py:62
  121.3 9.1 %convolution_bitcast_fusion = f32[32,1,48,2048]{3,2,0,1:T(8,128)} fusion(bf16[1,1024,2048]{2,1,0:T(8,128)(2,1)S(1)} %copy-done.2, bf16[32,48,1024]{2,1,0:T(8,128)(2,1)S(1)} %fusion), kind=kOutput, calls=%fused_computation.6 | convolution fusion | flops 6447169536 | bytes 19922944 | tf_op jit(solution)/shard_map/secf,efd->secd/dot_general | solution.py:66
  130.3 16.9 %reshape.151 = f32[1536,8,2,128]{3,2,1,0:T(2,128)} reshape(f32[32,1,48,2048]{3,2,0,1:T(8,128)} %convolution_bitcast_fusion) | data formatting | bytes 25165824 | tf_op jit(solution)/shard_map/reshape | solution.py:68
  147.2 13.8 %fusion.25 = (f32[1536,8,1,128]{3,2,1,0:T(1,128)S(1)}, f32[1536,8,1,128]{3,2,1,0:T(1,128)S(1)}) fusion(f32[1536,8,2,128]{3,2,1,0:T(2,128)} %reshape.151), kind=kLoop, calls=%fused_computation.85 | loop fusion | bytes 25165824 | tf_op jit(solution)/shard_map/slice | solution.py:70
  161.0 10.8 %constant_dynamic-slice_fusion.6 = (f32[1536,1,1,128]{3,2,1,0:T(1,128)S(1)}, f32[1536,1,1,128]{3,2,1,0:T(1,128)S(1)}, f32[1536,1,1,128]{3,2,1,0:T(1,128)S(1)}, f...) fusion(f32[1536,8,1,128]{3,2,1,0:T(1,128)S(1)} %get-tuple-eleme, ...), kind=kLoop, calls=%fused_computation.67 | loop fusion | bytes 25165888 | tf_op jit(solution)/shard_map/jit(dynamic_index_in_dim)/dynamic_slice | solution.py:27
  171.8 1.7 collective-permute-start
  173.6 4.0 %collective-permute-start.7 = (bf16[1536,128]{1,0:T(8,128)(2,1)S(1)}, bf16[1536,128]{1,0:T(8,128)(2,1)S(1)}, u32[]{:S(2)}, u32[]{:S(2)}) collective-permute-start(bf16[1536,128]{1,0:T(8,128)(2,1)S(1)} %convert_bitcast_fusion), channel_id=1, source_target_pairs={{0,7},{1,0},{2,1},{3,2},{4,3},{5,4},{6,5},{7,6},{8,15},{9,8},{10,9... | collective-permute-start | bytes 1179656 | tf_op jit(solution)/shard_map/ppermute | solution.py:31
  177.6 5.4 %collective-permute-done = bf16[1536,128]{1,0:T(8,128)(2,1)S(1)} collective-permute-done((bf16[1536,128]{1,0:T(8,128)(2,1)S(1)}, bf16[1536,128]{1,0:T(8,128)(2,1)S(1)}, u32[]{:S(2)}, u32[]{:S(2)}) %collective-permute-start) | collective-permute-done | bytes 393248 | tf_op jit(solution)/shard_map/ppermute | solution.py:31
  183.1 0.3 collective-permute-start.1
  183.5 2.7 collective-permute-start.8
  186.3 5.0 %collective-permute-done.1 = bf16[1536,128]{1,0:T(8,128)(2,1)S(1)} collective-permute-done((bf16[1536,128]{1,0:T(8,128)(2,1)S(1)}, bf16[1536,128]{1,0:T(8,128)(2,1)S(1)}, u32[]{:S(2)}, u32[]{:S(2)}) %collective-permute-start.1) | collective-permute-done | bytes 393248 | tf_op jit(solution)/shard_map/ppermute | solution.py:31
  191.5 2.7 collective-permute-start.9
  194.3 6.4 %collective-permute-done.2 = bf16[1536,128]{1,0:T(8,128)(2,1)S(1)} collective-permute-done((bf16[1536,128]{1,0:T(8,128)(2,1)S(1)}, bf16[1536,128]{1,0:T(8,128)(2,1)S(1)}, u32[]{:S(2)}, u32[]{:S(2)}) %collective-permute-start.2) | collective-permute-done | bytes 393248 | tf_op jit(solution)/shard_map/ppermute | solution.py:31
  201.0 3.0 collective-permute-start.10
  204.0 7.6 %collective-permute-done.3 = bf16[1536,128]{1,0:T(8,128)(2,1)S(1)} collective-permute-done((bf16[1536,128]{1,0:T(8,128)(2,1)S(1)}, bf16[1536,128]{1,0:T(8,128)(2,1)S(1)}, u32[]{:S(2)}, u32[]{:S(2)}) %collective-permute-start.3) | collective-permute-done | bytes 393248 | tf_op jit(solution)/shard_map/ppermute | solution.py:31
  211.8 3.0 collective-permute-start.11
  214.9 8.8 %collective-permute-done.4 = bf16[1536,128]{1,0:T(8,128)(2,1)S(1)} collective-permute-done((bf16[1536,128]{1,0:T(8,128)(2,1)S(1)}, bf16[1536,128]{1,0:T(8,128)(2,1)S(1)}, u32[]{:S(2)}, u32[]{:S(2)}) %collective-permute-start.4) | collective-permute-done | bytes 393248 | tf_op jit(solution)/shard_map/ppermute | solution.py:31
  224.0 3.0 collective-permute-start.12
  227.0 8.4 %collective-permute-done.5 = bf16[1536,128]{1,0:T(8,128)(2,1)S(1)} collective-permute-done((bf16[1536,128]{1,0:T(8,128)(2,1)S(1)}, bf16[1536,128]{1,0:T(8,128)(2,1)S(1)}, u32[]{:S(2)}, u32[]{:S(2)}) %collective-permute-start.5) | collective-permute-done | bytes 393248 | tf_op jit(solution)/shard_map/ppermute | solution.py:31
  235.6 3.0 collective-permute-start.13
  238.7 7.5 %collective-permute-done.6 = bf16[1536,128]{1,0:T(8,128)(2,1)S(1)} collective-permute-done((bf16[1536,128]{1,0:T(8,128)(2,1)S(1)}, bf16[1536,128]{1,0:T(8,128)(2,1)S(1)}, u32[]{:S(2)}, u32[]{:S(2)}) %collective-permute-start.6) | collective-permute-done | bytes 393248 | tf_op jit(solution)/shard_map/ppermute | solution.py:31
  246.3 1.2 pad_maximum_fusion
  247.6 17.4 %all-to-all-start.1 = ((f32[32,48,256]{2,1,0:T(8,128)}), f32[32,48,256]{2,1,0:T(8,128)S(1)}, u32[]{:S(2)}, u32[]{:S(2)}) async-start(f32[32,48,256]{2,1,0:T(8,128)} %bitcast.32), calls=%async_computation.1 | async-start | bytes 3145728 | tf_op jit(solution)/shard_map/all_to_all | solution.py:73
  265.0 2.3 select_reduce_fusion.1
  267.4 20.2 %all-to-all-done.1 = f32[32,48,256]{2,1,0:T(8,128)S(1)} async-done(((f32[32,48,256]{2,1,0:T(8,128)}), f32[32,48,256]{2,1,0:T(8,128)S(1)}, u32[]{:S(2)}, u32[]{:S(2)}) %all-to-all-start.1) | async-done | bytes 1572896 | tf_op jit(solution)/shard_map/all_to_all | solution.py:73
  287.6 3.5 %gather_fusion.1 = f32[1024,256]{1,0:T(8,128)S(1)} fusion(f32[1536,256]{1,0:T(8,128)S(1)} %bitcast.114, s32[1024]{0:T(1024)S(1)} %broadcast_clamp_fusion), kind=kCustom, calls=%fused_computation.1 | custom fusion | bytes 2101248 | tf_op jit(solution)/shard_map/gather | solution.py:82
  291.1 0.6 reshape.154
  291.7 0.8 fusion.26
  292.5 1.2 fusion.11
  293.7 1.9 collective-permute-start.14
  295.7 1.9 collective-permute-done.14
  297.6 0.2 fusion.19
  297.9 8.3 %collective-permute-done.15 = f32[256,256]{0,1:T(8,128)S(1)} collective-permute-done((f32[256,256]{0,1:T(8,128)S(1)}, f32[256,256]{0,1:T(8,128)S(1)}, u32[]{:S(2)}, u32[]{:S(2)}) %collective-permute-start.15) | collective-permute-done | bytes 262176 | tf_op jit(solution)/shard_map/ppermute | solution.py:40
  306.3 3.1 collective-permute-start.16
  309.3 11.9 %collective-permute-done.16 = f32[256,256]{0,1:T(8,128)S(1)} collective-permute-done((f32[256,256]{0,1:T(8,128)S(1)}, f32[256,256]{0,1:T(8,128)S(1)}, u32[]{:S(2)}, u32[]{:S(2)}) %collective-permute-start.16) | collective-permute-done | bytes 262176 | tf_op jit(solution)/shard_map/ppermute | solution.py:40
  321.3 3.3 collective-permute-start.17
  325.3 13.7 %collective-permute-done.17 = f32[256,256]{0,1:T(8,128)S(1)} collective-permute-done((f32[256,256]{0,1:T(8,128)S(1)}, f32[256,256]{0,1:T(8,128)S(1)}, u32[]{:S(2)}, u32[]{:S(2)}) %collective-permute-start.17) | collective-permute-done | bytes 262176 | tf_op jit(solution)/shard_map/ppermute | solution.py:40
  339.2 0.2 fusion.7
  339.4 0.7 pad_maximum_fusion.1
  (59 shorter events, 3.2 us)
Async XLA Ops:
  0.0 265.0 %copy-start = (bf16[2048,32]{0,1:T(8,128)(2,1)S(1)}, bf16[2048,32]{0,1:T(8,128)(2,1)}, u32[]{:S(2)}) copy-start(bf16[2048,32]{0,1:T(8,128)(2,1)} %param.7) | copy-start | bytes 393220
  25.2 85.9 %all-to-all-start = ((bf16[32,1,48,2048]{3,2,1,0:T(8,128)(2,1)}), bf16[32,1,48,2048]{3,2,1,0:T(8,128)(2,1)}, u32[]{:S(2)}, u32[]{:S(2)}) async-start(bf16[32,1,48,2048]{3,2,1,0:T(8,128)(2,1)} %bitcast.115), calls=%async_computation | async-start | bytes 12582912 | tf_op jit(solution)/shard_map/all_to_all | solution.py:61
  111.1 10.1 %copy-start.2 = (bf16[1,1024,2048]{2,1,0:T(8,128)(2,1)S(1)}, bf16[1,1024,2048]{2,1,0:T(8,128)(2,1)}, u32[]{:S(2)}) copy-start(bf16[1,1024,2048]{2,1,0:T(8,128)(2,1)} %param.9) | copy-start | bytes 12582916
  171.8 11.2 %collective-permute-start = (bf16[1536,128]{1,0:T(8,128)(2,1)S(1)}, bf16[1536,128]{1,0:T(8,128)(2,1)S(1)}, u32[]{:S(2)}, u32[]{:S(2)}) collective-permute-start(bf16[1536,128]{1,0:T(8,128)(2,1)S(1)} %convert_bitcast_fusion.1), channel_id=1, source_target_pairs={{0,1},{1,2},{2,3},{3,4},{4,5},{5,6},{6,7},{7,0},{8,9},{9,10},{10,1... | collective-permute-start | bytes 1179656 | tf_op jit(solution)/shard_map/ppermute | solution.py:31
  173.6 9.9 %collective-permute-start.7 = (bf16[1536,128]{1,0:T(8,128)(2,1)S(1)}, bf16[1536,128]{1,0:T(8,128)(2,1)S(1)}, u32[]{:S(2)}, u32[]{:S(2)}) collective-permute-start(bf16[1536,128]{1,0:T(8,128)(2,1)S(1)} %convert_bitcast_fusion), channel_id=1, source_target_pairs={{0,7},{1,0},{2,1},{3,2},{4,3},{5,4},{6,5},{7,6},{8,15},{9,8},{10,9... | collective-permute-start | bytes 1179656 | tf_op jit(solution)/shard_map/ppermute | solution.py:31
  183.1 8.1 %collective-permute-start.1 = (bf16[1536,128]{1,0:T(8,128)(2,1)S(1)}, bf16[1536,128]{1,0:T(8,128)(2,1)S(1)}, u32[]{:S(2)}, u32[]{:S(2)}) collective-permute-start(bf16[1536,128]{1,0:T(8,128)(2,1)S(1)} %add_convert_fusion.11), channel_id=1, source_target_pairs={{0,1},{1,2},{2,3},{3,4},{4,5},{5,6},{6,7},{7,0},{8,9},{9,10},{10,1... | collective-permute-start | bytes 1179656 | tf_op jit(solution)/shard_map/ppermute | solution.py:31
  183.5 7.9 %collective-permute-start.8 = (bf16[1536,128]{1,0:T(8,128)(2,1)S(1)}, bf16[1536,128]{1,0:T(8,128)(2,1)S(1)}, u32[]{:S(2)}, u32[]{:S(2)}) collective-permute-start(bf16[1536,128]{1,0:T(8,128)(2,1)S(1)} %add_convert_fusion.5), channel_id=1, source_target_pairs={{0,7},{1,0},{2,1},{3,2},{4,3},{5,4},{6,5},{7,6},{8,15},{9,8},{10,9... | collective-permute-start | bytes 1179656 | tf_op jit(solution)/shard_map/ppermute | solution.py:31
  191.3 9.3 %collective-permute-start.2 = (bf16[1536,128]{1,0:T(8,128)(2,1)S(1)}, bf16[1536,128]{1,0:T(8,128)(2,1)S(1)}, u32[]{:S(2)}, u32[]{:S(2)}) collective-permute-start(bf16[1536,128]{1,0:T(8,128)(2,1)S(1)} %add_convert_fusion.10), channel_id=1, source_target_pairs={{0,1},{1,2},{2,3},{3,4},{4,5},{5,6},{6,7},{7,0},{8,9},{9,10},{10,1... | collective-permute-start | bytes 1179656 | tf_op jit(solution)/shard_map/ppermute | solution.py:31
  191.5 9.3 %collective-permute-start.9 = (bf16[1536,128]{1,0:T(8,128)(2,1)S(1)}, bf16[1536,128]{1,0:T(8,128)(2,1)S(1)}, u32[]{:S(2)}, u32[]{:S(2)}) collective-permute-start(bf16[1536,128]{1,0:T(8,128)(2,1)S(1)} %add_convert_fusion.4), channel_id=1, source_target_pairs={{0,7},{1,0},{2,1},{3,2},{4,3},{5,4},{6,5},{7,6},{8,15},{9,8},{10,9... | collective-permute-start | bytes 1179656 | tf_op jit(solution)/shard_map/ppermute | solution.py:31
  200.8 10.8 %collective-permute-start.3 = (bf16[1536,128]{1,0:T(8,128)(2,1)S(1)}, bf16[1536,128]{1,0:T(8,128)(2,1)S(1)}, u32[]{:S(2)}, u32[]{:S(2)}) collective-permute-start(bf16[1536,128]{1,0:T(8,128)(2,1)S(1)} %add_convert_fusion.9), channel_id=1, source_target_pairs={{0,1},{1,2},{2,3},{3,4},{4,5},{5,6},{6,7},{7,0},{8,9},{9,10},{10,1... | collective-permute-start | bytes 1179656 | tf_op jit(solution)/shard_map/ppermute | solution.py:31
  201.0 10.8 %collective-permute-start.10 = (bf16[1536,128]{1,0:T(8,128)(2,1)S(1)}, bf16[1536,128]{1,0:T(8,128)(2,1)S(1)}, u32[]{:S(2)}, u32[]{:S(2)}) collective-permute-start(bf16[1536,128]{1,0:T(8,128)(2,1)S(1)} %add_convert_fusion.3), channel_id=1, source_target_pairs={{0,7},{1,0},{2,1},{3,2},{4,3},{5,4},{6,5},{7,6},{8,15},{9,8},{10,9... | collective-permute-start | bytes 1179656 | tf_op jit(solution)/shard_map/ppermute | solution.py:31
  211.7 12.1 %collective-permute-start.4 = (bf16[1536,128]{1,0:T(8,128)(2,1)S(1)}, bf16[1536,128]{1,0:T(8,128)(2,1)S(1)}, u32[]{:S(2)}, u32[]{:S(2)}) collective-permute-start(bf16[1536,128]{1,0:T(8,128)(2,1)S(1)} %add_convert_fusion.8), channel_id=1, source_target_pairs={{0,1},{1,2},{2,3},{3,4},{4,5},{5,6},{6,7},{7,0},{8,9},{9,10},{10,1... | collective-permute-start | bytes 1179656 | tf_op jit(solution)/shard_map/ppermute | solution.py:31
  211.8 12.0 %collective-permute-start.11 = (bf16[1536,128]{1,0:T(8,128)(2,1)S(1)}, bf16[1536,128]{1,0:T(8,128)(2,1)S(1)}, u32[]{:S(2)}, u32[]{:S(2)}) collective-permute-start(bf16[1536,128]{1,0:T(8,128)(2,1)S(1)} %add_convert_fusion.2), channel_id=1, source_target_pairs={{0,7},{1,0},{2,1},{3,2},{4,3},{5,4},{6,5},{7,6},{8,15},{9,8},{10,9... | collective-permute-start | bytes 1179656 | tf_op jit(solution)/shard_map/ppermute | solution.py:31
  223.8 11.6 %collective-permute-start.5 = (bf16[1536,128]{1,0:T(8,128)(2,1)S(1)}, bf16[1536,128]{1,0:T(8,128)(2,1)S(1)}, u32[]{:S(2)}, u32[]{:S(2)}) collective-permute-start(bf16[1536,128]{1,0:T(8,128)(2,1)S(1)} %add_convert_fusion.7), channel_id=1, source_target_pairs={{0,1},{1,2},{2,3},{3,4},{4,5},{5,6},{6,7},{7,0},{8,9},{9,10},{10,1... | collective-permute-start | bytes 1179656 | tf_op jit(solution)/shard_map/ppermute | solution.py:31
  224.0 11.6 %collective-permute-start.12 = (bf16[1536,128]{1,0:T(8,128)(2,1)S(1)}, bf16[1536,128]{1,0:T(8,128)(2,1)S(1)}, u32[]{:S(2)}, u32[]{:S(2)}) collective-permute-start(bf16[1536,128]{1,0:T(8,128)(2,1)S(1)} %add_convert_fusion.1), channel_id=1, source_target_pairs={{0,7},{1,0},{2,1},{3,2},{4,3},{5,4},{6,5},{7,6},{8,15},{9,8},{10,9... | collective-permute-start | bytes 1179656 | tf_op jit(solution)/shard_map/ppermute | solution.py:31
  235.4 10.7 %collective-permute-start.6 = (bf16[1536,128]{1,0:T(8,128)(2,1)S(1)}, bf16[1536,128]{1,0:T(8,128)(2,1)S(1)}, u32[]{:S(2)}, u32[]{:S(2)}) collective-permute-start(bf16[1536,128]{1,0:T(8,128)(2,1)S(1)} %add_convert_fusion.6), channel_id=1, source_target_pairs={{0,1},{1,2},{2,3},{3,4},{4,5},{5,6},{6,7},{7,0},{8,9},{9,10},{10,1... | collective-permute-start | bytes 1179656 | tf_op jit(solution)/shard_map/ppermute | solution.py:31
  235.6 10.6 %collective-permute-start.13 = (bf16[1536,128]{1,0:T(8,128)(2,1)S(1)}, bf16[1536,128]{1,0:T(8,128)(2,1)S(1)}, u32[]{:S(2)}, u32[]{:S(2)}) collective-permute-start(bf16[1536,128]{1,0:T(8,128)(2,1)S(1)} %add_convert_fusion), channel_id=1, source_target_pairs={{0,7},{1,0},{2,1},{3,2},{4,3},{5,4},{6,5},{7,6},{8,15},{9,8},{10,9... | collective-permute-start | bytes 1179656 | tf_op jit(solution)/shard_map/ppermute | solution.py:31
  246.2 18.7 %copy-start.1 = (s32[512,2]{0,1:T(2,128)S(1)}, s32[512,2]{0,1:T(2,128)}, u32[]{:S(2)}) copy-start(s32[512,2]{0,1:T(2,128)} %param.10) | copy-start | bytes 12292
  247.6 40.1 %all-to-all-start.1 = ((f32[32,48,256]{2,1,0:T(8,128)}), f32[32,48,256]{2,1,0:T(8,128)S(1)}, u32[]{:S(2)}, u32[]{:S(2)}) async-start(f32[32,48,256]{2,1,0:T(8,128)} %bitcast.32), calls=%async_computation.1 | async-start | bytes 3145728 | tf_op jit(solution)/shard_map/all_to_all | solution.py:73
  293.7 3.9 %collective-permute-start.14 = (bf16[256,256]{1,0:T(8,128)(2,1)S(1)}, bf16[256,256]{1,0:T(8,128)(2,1)S(1)}, u32[]{:S(2)}, u32[]{:S(2)}) collective-permute-start(bf16[256,256]{1,0:T(8,128)(2,1)S(1)} %slice.52), channel_id=1, source_target_pairs={{0,8},{8,16},{16,24},{24,32},{32,40},{40,48},{48,56},{56,64},{64,7... | collective-permute-start | bytes 393224 | tf_op jit(solution)/shard_map/ppermute | solution.py:17
  297.8 8.4 %collective-permute-start.15 = (f32[256,256]{0,1:T(8,128)S(1)}, f32[256,256]{0,1:T(8,128)S(1)}, u32[]{:S(2)}, u32[]{:S(2)}) collective-permute-start(f32[256,256]{0,1:T(8,128)S(1)} %fusion.19), channel_id=1, source_target_pairs={{0,1},{1,0},{2,3},{3,2},{4,5},{5,4},{6,7},{7,6},{8,9},{9,8},{10,11... | collective-permute-start | bytes 786440 | tf_op jit(solution)/shard_map/ppermute | solution.py:40
  306.3 15.0 %collective-permute-start.16 = (f32[256,256]{0,1:T(8,128)S(1)}, f32[256,256]{0,1:T(8,128)S(1)}, u32[]{:S(2)}, u32[]{:S(2)}) collective-permute-start(f32[256,256]{0,1:T(8,128)S(1)} %add.376), channel_id=1, source_target_pairs={{0,2},{1,3},{2,0},{3,1},{4,6},{5,7},{6,4},{7,5},{8,10},{9,11},{10,... | collective-permute-start | bytes 786440 | tf_op jit(solution)/shard_map/ppermute | solution.py:40
  321.3 17.7 %collective-permute-start.17 = (f32[256,256]{0,1:T(8,128)S(1)}, f32[256,256]{0,1:T(8,128)S(1)}, u32[]{:S(2)}, u32[]{:S(2)}) collective-permute-start(f32[256,256]{0,1:T(8,128)S(1)} %add.377), channel_id=1, source_target_pairs={{0,4},{1,5},{2,6},{3,7},{4,0},{5,1},{6,2},{7,3},{8,12},{9,13},{10,... | collective-permute-start | bytes 786440 | tf_op jit(solution)/shard_map/ppermute | solution.py:40
